TPU v7x, 128 devices: a whole 4x4x4 slice. The times are simulated.
128 devices in a mesh: chan: 4 (over z_lo, core), blk: 32 (over z_hi, y, x).
Axes of the slice: x: 4, y: 4, z: 4 (z_hi: 2, z_lo: 2; z = z_hi * 2 + z_lo), core: 2. Of those that a mesh axis runs over, the one named last changes fastest.
Arguments:
- voltages: bfloat16 [256, 262144], P('blk', 'chan'), may hold values from -6 to 6
- fir_taps: float32 [8, 4096], replicated, may hold values from -2.1 to 2.1
Outputs:
- visibilities: float32 [2, 256, 256, 2048], P(None, 'blk', None, 'chan')
All inputs are finite; a program needn't handle non-finite values.
Results may differ from a plain program's by a relative error of at most 0.0036.
Values may be sent and summed in bfloat16 or wider, within the bound.
No kernel may reach another device: no remote copies, remote signals or barrier semaphores. Data moves between devices by JAX's collectives and lax.ppermute only.
A program may use at most 192 MiB of HBM per device.

v0:
```python
import math
import jax
import jax.numpy as jnp
from jax import lax
from jax.sharding import PartitionSpec as P

TAPS = 8
L = 4096
C = 2048


def shifted(value, axis, steps):
    count = lax.axis_size(axis)
    leading, last = (max(0, -steps), min(count, count - steps))
    return lax.ppermute(value, axis, [(source, source + steps) for source in range(leading, last)])


def dft_table(first_channel, channel_count, length):
    channel_ids = first_channel + jnp.arange(channel_count, dtype=jnp.int32)
    sample_ids = jnp.arange(length, dtype=jnp.int32)
    phase_index = sample_ids[:, None] * channel_ids[None, :] % length
    angles = phase_index.astype(jnp.float32) * (2.0 * math.pi / length)
    normaliser = 1.0 / math.sqrt(length)
    return jnp.concatenate([jnp.cos(angles) * normaliser, -jnp.sin(angles) * normaliser], axis=1)


def correlate_pair(left_block, right_block, inverse_count):
    gram_terms = jnp.einsum(
        "itpc,jtqc->ipjqc", left_block, right_block, preferred_element_type=jnp.float32
    )
    real_part = gram_terms[:, 0, :, 0] + gram_terms[:, 1, :, 1]
    imag_part = gram_terms[:, 1, :, 0] - gram_terms[:, 0, :, 1]
    return jnp.stack([real_part, imag_part]) * inverse_count


def on_device(voltages, fir_taps):
    feed_count = voltages.shape[0]
    frame_count = voltages.shape[1] // L
    own_frames = voltages.reshape(feed_count, frame_count, L)
    last_frames = own_frames[:, frame_count - (TAPS - 1) :, :]
    earlier = shifted(last_frames, "chan", 1)
    extended = jnp.concatenate([earlier, own_frames], axis=1)
    filtered = jnp.zeros((feed_count, frame_count, L), jnp.float32)
    for tap_index in range(TAPS):
        filtered = filtered + fir_taps[tap_index][None, None, :] * extended[
            :, tap_index : tap_index + frame_count, :
        ].astype(jnp.float32)
    frame_rows = filtered.reshape(feed_count * frame_count, L)
    block_width = min(C, 512)
    pieces = []
    for first_channel in range(0, C, block_width):
        cos_sin_table = dft_table(first_channel, block_width, L)
        product = jnp.dot(
            frame_rows,
            cos_sin_table,
            precision=lax.Precision.HIGHEST,
            preferred_element_type=jnp.float32,
        )
        pieces.append(product.reshape(feed_count * frame_count, 2, block_width))
    spectra = (
        jnp.concatenate(pieces, axis=2).astype(jnp.bfloat16).reshape(feed_count, frame_count, 2, C)
    )
    own_block = lax.all_to_all(spectra, "chan", split_axis=3, concat_axis=1, tiled=True)
    inverse_count = 1.0 / own_block.shape[1]
    return correlate_pair(
        own_block, lax.all_gather(own_block, "blk", axis=0, tiled=True), inverse_count
    )


def solution(mesh):
    placed = (P("blk", "chan"), P())
    return jax.shard_map(
        on_device,
        mesh=mesh,
        in_specs=placed,
        out_specs=P(None, "blk", None, "chan"),
        check_vma=False,
    )
```

profile of v0, /device:TPU:0, one launch (start us, length us, event | category | flops | bytes accessed | tf_op | source)
XLA Modules:
  0.0 1170.2 jit_solution(16669685366088658176)
XLA Ops:
  6.5 1.8 copy.28
  8.3 0.1 slice.80
  8.5 2.1 collective-permute-start
  10.6 33.0 %negate_multiply_fusion.3 = (f32[4096,512]{0,1:T(8,128)S(1)}, f32[4096,512]{0,1:T(8,128)S(1)}) fusion(), kind=kLoop, calls=%fused_computation.44 | loop fusion | flops 35651584 | bytes 16777216 | tf_op jit(solution)/shard_map/mul | solution.py:24
  43.6 0.1 fusion.58
  43.7 33.8 %cosine_multiply_fusion = (f32[4096,512]{0,1:T(8,128)S(1)}, f32[4096,512]{0,1:T(8,128)S(1)}) fusion(s32[512]{0:T(512)S(1)} %iota_add_fusion), kind=kLoop, calls=%fused_computation.33 | loop fusion | flops 35651584 | bytes 16779264 | tf_op jit(solution)/shard_map/mul | solution.py:24
  77.5 37.2 %cosine_multiply_fusion.1 = (f32[4096,512]{0,1:T(8,128)}, f32[4096,512]{0,1:T(8,128)}) fusion(s32[512]{0:T(512)S(1)} %iota_add_fusion.1), kind=kLoop, calls=%fused_computation.37 | loop fusion | flops 35651584 | bytes 16779264 | tf_op jit(solution)/shard_map/mul | solution.py:24
  114.7 37.2 %cosine_multiply_fusion.2 = (f32[4096,512]{0,1:T(8,128)}, f32[4096,512]{0,1:T(8,128)}) fusion(s32[512]{0:T(512)S(1)} %iota_add_fusion.2), kind=kLoop, calls=%fused_computation.41 | loop fusion | flops 35651584 | bytes 16779264 | tf_op jit(solution)/shard_map/mul | solution.py:24
  151.9 6.2 pad_maximum_fusion.3
  158.2 13.7 %pad_maximum_fusion.2 = f32[4096,1024]{0,1:T(8,128)} fusion(f32[4096,512]{0,1:T(8,128)} %get-tuple-element.16, f32[4096,512]{0,1:T(8,128)} %get-tuple-element.15), kind=kLoop, calls=%fused_computation.4 | loop fusion | flops 4194304 | bytes 33554432 | tf_op jit(solution)/shard_map/concatenate | solution.py:24
  171.9 0.0 copy-done
  171.9 2.7 copy-done.1
  174.6 6.4 pad_maximum_fusion.1
  181.0 6.2 pad_maximum_fusion
  187.3 0.0 collective-permute-done
  187.3 5.8 multiply_add_fusion
  193.1 0.0 copy-start.2
  193.1 0.0 slice-start.1
  193.2 0.0 slice-start.2
  193.2 0.0 slice-start.3
  193.2 22.5 %fusion.49 = bf16[8,16,2,512]{3,1,2,0:T(8,128)(2,1)} fusion(f32[2,512,4096,1]{2,1,0,3:T(8,128)} %bitcast.85, f32[8,16,4096]{2,1,0:T(8,128)S(1)} %multiply_add_fusion), kind=kOutput, calls=%fused_computation.82 | convolution fusion | flops 6442582016 | bytes 19136512 | tf_op jit(solution)/shard_map/dot_general | solution.py:53
  215.7 0.0 copy-done.2
  215.7 0.0 slice-done
  215.7 0.0 slice-done.1
  215.7 0.0 slice-done.2
  215.7 0.0 slice-done.3
  215.7 0.0 copy-start.3
  215.7 0.0 slice-start.4
  215.7 0.0 slice-start.5
  215.8 20.0 %fusion.46 = bf16[8,16,2,512]{3,1,2,0:T(8,128)(2,1)} fusion(f32[2,512,4096,1]{2,1,0,3:T(8,128)S(1)} %bitcast.88, f32[8,16,4096]{2,1,0:T(8,128)} %copy-done.2), kind=kOutput, calls=%fused_computation.81 | convolution fusion | flops 6442582016 | bytes 19136512 | tf_op jit(solution)/shard_map/dot_general | solution.py:53
  235.7 20.8 %fusion.43 = bf16[8,16,2,512]{3,1,2,0:T(8,128)(2,1)S(1)} fusion(f32[2,512,4096,1]{2,1,0,3:T(8,128)} %bitcast.89, f32[8,16,4096]{2,1,0:T(8,128)S(1)} %copy-done.3), kind=kOutput, calls=%fused_computation.80 | convolution fusion | flops 6442582016 | bytes 19136512 | tf_op jit(solution)/shard_map/dot_general | solution.py:53
  256.6 17.6 %fusion.40 = bf16[8,16,2,512]{3,1,2,0:T(8,128)(2,1)S(1)} fusion(f32[2,512,4096,1]{2,1,0,3:T(8,128)S(1)} %bitcast.92, f32[8,16,4096]{2,1,0:T(8,128)S(1)} %copy-done.3), kind=kOutput, calls=%fused_computation.79 | convolution fusion | flops 6442582016 | bytes 19136512 | tf_op jit(solution)/shard_map/dot_general | solution.py:53
  274.2 0.1 pad_maximum_fusion.5
  274.4 14.3 %copy.31 = bf16[8,16,2,2048]{1,2,0,3:T(2,128)(2,1)} copy(bf16[8,16,2,2048]{3,1,2,0:T(8,128)(2,1)S(1)} %pad_maximum_fusion.5) | data formatting | bytes 2097152 | tf_op jit(solution)/shard_map/concatenate | solution.py:61
  288.7 10.2 reshape.89
  298.9 17.5 %all_to_all.18 = bf16[4,2,65536]{2,1,0:T(2,128)(2,1)S(1)} all-to-all(bf16[4,2,65536]{2,1,0:T(2,128)(2,1)S(1)} %reshape.89), channel_id=1, replica_groups=mesh['chan'=4,'blk'=32] {'chan'}, dimensions={0} | all-to-all | bytes 2097152 | tf_op jit(solution)/shard_map/all_to_all | solution.py:63
  316.4 7.1 reshape.90
  323.5 19.1 %copy.42 = bf16[8,16,2,4,512]{4,3,1,2,0:T(4,128)(2,1)S(1)} copy(bf16[8,16,2,4,512]{1,2,0,4,3:T(2,128)(2,1)} %bitcast.84) | data formatting | bytes 2097152 | tf_op jit(solution)/shard_map/all_to_all | solution.py:63
  342.6 0.2 copy.33
  342.9 2.8 copy.34
  345.7 0.0 all-gather.2.cloned.1.call-update
  345.7 2.0 copy.41
  347.8 761.5 %all-gather.2.cloned.1.call-done = bf16[256,64,2,512]{1,0,2,3:T(8,128)(2,1)} async-done(((bf16[8,64,2,512]{1,0,2,3:T(8,128)(2,1)}), bf16[256,64,2,512]{1,0,2,3:T(8,128)(2,1)}) %all-gather.2.cloned.1.call-update) | async-done | bytes 33554448 | tf_op jit(solution)/shard_map/all_gather | solution.py:66
  1109.2 32.0 %fusion.2 = f32[8,2,256,2,512]{2,0,1,3,4:T(8,128)} fusion(bf16[8,64,2,512,1]{1,0,2,4,3:T(8,128)(2,1)S(1)} %copy.41, bf16[256,64,2,512]{1,0,2,3:T(8,128)(2,1)} %all-gather.2.cloned.1.call-done), kind=kOutput, calls=%fused_computation.18 | convolution fusion | flops 536870912 | bytes 51380224 | tf_op jit(solution)/shard_map/itpc,jtqc->ipjqc/dot_general | solution.py:28
  1141.2 4.0 fusion.29
  1145.2 4.0 fusion.31
  1149.2 3.8 maximum_multiply_fusion
  1153.0 9.9 copy.38
  (22 shorter events, 0.0 us)
Async XLA Ops:
  6.5 1102.7 %all-gather.2.cloned.1.call-start = ((), (), s32[]{:S(2)}) async-start(), calls=%async_computation.1 | async-start | bytes 69206016 | tf_op jit(solution)/shard_map/all_gather | solution.py:66
  8.5 178.8 %collective-permute-start = (bf16[8,7,4096]{2,1,0:T(8,128)(2,1)S(1)}, bf16[8,7,4096]{2,1,0:T(8,128)(2,1)}, u32[]{:S(2)}, u32[]{:S(2)}) collective-permute-start(bf16[8,7,4096]{2,1,0:T(8,128)(2,1)S(1)} %slice.80), channel_id=1, source_target_pairs={{0,32},{32,64},{64,96},{1,33},{33,65},{65,97},{2,34},{34,66},{66,9... | collective-permute-start | bytes 1376264 | tf_op jit(solution)/shard_map/ppermute | solution.py:15
  10.6 33.0 %copy-start.6 = (f32[8,4096]{1,0:T(8,128)S(1)}, f32[8,4096]{1,0:T(8,128)}, u32[]{:S(2)}) copy-start(f32[8,4096]{1,0:T(8,128)} %param.3) | copy-start | bytes 393220
  158.2 13.7 %copy-start = (f32[4096,512]{0,1:T(8,128)S(1)}, f32[4096,512]{0,1:T(8,128)}, u32[]{:S(2)}) copy-start(f32[4096,512]{0,1:T(8,128)} %get-tuple-element.13) | copy-start | bytes 25165828
  158.2 16.5 %copy-start.1 = (f32[4096,512]{0,1:T(8,128)S(1)}, f32[4096,512]{0,1:T(8,128)}, u32[]{:S(2)}) copy-start(f32[4096,512]{0,1:T(8,128)} %get-tuple-element.14) | copy-start | bytes 25165828
  187.3 28.4 %slice-start = ((s8[16777216]{0:T(1024)(128)(4,1)}), s8[4194304]{0:T(1024)(128)(4,1)S(1)}, s32[]{:S(2)}) async-start(s8[16777216]{0:T(1024)(128)(4,1)} %bitcast.86), calls=%async_computation.2 | async-start | bytes 8388608
  193.1 22.5 %copy-start.2 = (f32[8,16,4096]{2,1,0:T(8,128)}, f32[8,16,4096]{2,1,0:T(8,128)S(1)}, u32[]{:S(2)}) copy-start(f32[8,16,4096]{2,1,0:T(8,128)S(1)} %multiply_add_fusion) | copy-start | bytes 6291460
  193.1 22.5 %slice-start.1 = ((s8[16777216]{0:T(1024)(128)(4,1)}), s8[4194304]{0:T(1024)(128)(4,1)S(1)}, s32[]{:S(2)}) async-start(s8[16777216]{0:T(1024)(128)(4,1)} %bitcast.86), calls=%async_computation.3 | async-start | bytes 8388608
  193.2 22.5 %slice-start.2 = ((s8[16777216]{0:T(1024)(128)(4,1)}), s8[4194304]{0:T(1024)(128)(4,1)S(1)}, s32[]{:S(2)}) async-start(s8[16777216]{0:T(1024)(128)(4,1)} %bitcast.86), calls=%async_computation.4 | async-start | bytes 8388608
  193.2 22.5 %slice-start.3 = ((s8[16777216]{0:T(1024)(128)(4,1)}), s8[4194304]{0:T(1024)(128)(4,1)S(1)}, s32[]{:S(2)}) async-start(s8[16777216]{0:T(1024)(128)(4,1)} %bitcast.86), calls=%async_computation.5 | async-start | bytes 8388608
  215.7 20.0 %copy-start.3 = (f32[8,16,4096]{2,1,0:T(8,128)S(1)}, f32[8,16,4096]{2,1,0:T(8,128)}, u32[]{:S(2)}) copy-start(f32[8,16,4096]{2,1,0:T(8,128)} %copy-done.2) | copy-start | bytes 6291460
  215.7 40.8 %slice-start.4 = ((s8[16777216]{0:T(1024)(128)(4,1)}), s8[4194304]{0:T(1024)(128)(4,1)S(1)}, s32[]{:S(2)}) async-start(s8[16777216]{0:T(1024)(128)(4,1)} %bitcast.90), calls=%async_computation.6 | async-start | bytes 8388608
  215.7 40.8 %slice-start.5 = ((s8[16777216]{0:T(1024)(128)(4,1)}), s8[4194304]{0:T(1024)(128)(4,1)S(1)}, s32[]{:S(2)}) async-start(s8[16777216]{0:T(1024)(128)(4,1)} %bitcast.90), calls=%async_computation.7 | async-start | bytes 8388608
  235.7 20.8 %slice-start.6 = ((s8[16777216]{0:T(1024)(128)(4,1)}), s8[4194304]{0:T(1024)(128)(4,1)S(1)}, s32[]{:S(2)}) async-start(s8[16777216]{0:T(1024)(128)(4,1)} %bitcast.90), calls=%async_computation.8 | async-start | bytes 8388608
  235.7 20.8 %slice-start.7 = ((s8[16777216]{0:T(1024)(128)(4,1)}), s8[4194304]{0:T(1024)(128)(4,1)S(1)}, s32[]{:S(2)}) async-start(s8[16777216]{0:T(1024)(128)(4,1)} %bitcast.90), calls=%async_computation.9 | async-start | bytes 8388608
  256.6 17.6 %copy-start.4 = (bf16[8,16,2,512]{3,1,2,0:T(8,128)(2,1)S(1)}, bf16[8,16,2,512]{3,1,2,0:T(8,128)(2,1)}, u32[]{:S(2)}) copy-start(bf16[8,16,2,512]{3,1,2,0:T(8,128)(2,1)} %fusion.49) | copy-start | bytes 786436
  256.6 17.6 %copy-start.5 = (bf16[8,16,2,512]{3,1,2,0:T(8,128)(2,1)S(1)}, bf16[8,16,2,512]{3,1,2,0:T(8,128)(2,1)}, u32[]{:S(2)}) copy-start(bf16[8,16,2,512]{3,1,2,0:T(8,128)(2,1)} %fusion.46) | copy-start | bytes 786436
Sparse Core Ops, SparseCore 0:
  345.8 763.3 all-gather.1
where the time goes:
time: 1180 us; the launch traced here: 1170 us
  waiting for transfers between devices  761 us (64%)
  other arithmetic  192 us (16%)
  matrix products  113 us (10%)
  local copies, waits for them, and re-layouts  70.6 us (6%)
  blocking collectives  17.5 us (1%)
  between operations  14.1 us (1%)
    all_gather x1, waiting for transfers between devices, on_device(): lax.all_gather(own_block, 'blk', axis=0, tiled=True)  761 us
    mul x3, other arithmetic, dft_table(): jnp.cos(angles) * normaliser  108 us
    dot_general x4, matrix products, on_device(): jnp.dot(frame_rows, cos_sin_table, precision=lax.Precision.HIGHEST, prefe...  80.8 us
    mul x1, other arithmetic, dft_table(): -jnp.sin(angles) * normaliser  33 us
    concatenate x4, other arithmetic, dft_table(): jnp.concatenate([jnp.cos(angles) * normaliser, -jnp.sin(angles) * normali...  32.6 us
    dot_general x1, matrix products, correlate_pair(): jnp.einsum('itpc,jtqc->ipjqc', left_block, right_block, preferred_element...  32 us
    all_to_all x4, local copies, waits for them, and re-layouts, on_device(): lax.all_to_all(spectra, 'chan', split_axis=3, concat_axis=1, tiled=True)  24.2 us
  transfers between devices with their start and end apart: 2, of which 1 were waited for; matrix products, arithmetic and copies ran while one was open for 15% of the time, Pallas kernels for 0%

commit v1 on v0

--- a/solution.py
+++ b/solution.py
@@ -1,3 +1,4 @@
+import functools
 import math
 import jax
 import jax.numpy as jnp
@@ -7,6 +8,21 @@
 TAPS = 8
 L = 4096
 C = 2048
+
+
+def update_rows(body, group_axis):
+    return jnp.concatenate(
+        lax.all_to_all(
+            jnp.stack(tuple((body for _ in range(lax.axis_size(group_axis)))), axis=0),
+            axis_name=group_axis,
+            split_axis=0,
+            concat_axis=0,
+        ),
+        0,
+    )
+
+
+_bring_block = functools.partial(update_rows, group_axis="blk")
 
 
 def shifted(value, axis, steps):
@@ -62,9 +78,7 @@
     )
     own_block = lax.all_to_all(spectra, "chan", split_axis=3, concat_axis=1, tiled=True)
     inverse_count = 1.0 / own_block.shape[1]
-    return correlate_pair(
-        own_block, lax.all_gather(own_block, "blk", axis=0, tiled=True), inverse_count
-    )
+    return correlate_pair(own_block, _bring_block(own_block), inverse_count)
 
 
 def solution(mesh):

time: 1180 us -> 1100 us (0.932)
  the two profiles are of different devices: /device:TPU:0 before, /device:TPU:40 now
where the time goes in v1:
time: 1100 us; the launch traced here: 1090 us
  waiting for transfers between devices  630 us (57%)
  other arithmetic  206 us (19%)
  local copies, waits for them, and re-layouts  127 us (12%)
  matrix products  99.7 us (9%)
  blocking collectives  15.8 us (1%)
  starting transfers between devices  12.2 us (1%)
    all_to_all x1, waiting for transfers between devices, update_rows(): lax.all_to_all(jnp.stack(tuple((body for _ in range(lax.axis_size(group_a...  630 us
    mul x3, other arithmetic, dft_table(): jnp.cos(angles) * normaliser  119 us
    dot_general x4, matrix products, on_device(): jnp.dot(frame_rows, cos_sin_table, precision=lax.Precision.HIGHEST, prefe...  80.8 us
    reshape x1, local copies, waits for them, and re-layouts, update_rows(): jnp.concatenate(lax.all_to_all(jnp.stack(tuple((body for _ in range(lax.a...  50.8 us
    concatenate x4, other arithmetic, dft_table(): jnp.concatenate([jnp.cos(angles) * normaliser, -jnp.sin(angles) * normali...  36.6 us
    mul x1, other arithmetic, dft_table(): -jnp.sin(angles) * normaliser  33 us
  transfers between devices with their start and end apart: 2, of which 1 were waited for; matrix products, arithmetic and copies ran while one was open for 17% of the time, Pallas kernels for 0%

profile of v1, /device:TPU:40, one launch (start us, length us, event | category | flops | bytes accessed | tf_op | source)
XLA Modules:
  0.0 1091.1 jit_solution(1122099602776420384)
XLA Ops:
  0.0 1.8 copy.29
  1.8 0.1 slice.80
  1.9 1.9 collective-permute-start
  3.9 0.0 copy-start.4
  3.9 33.0 %negate_multiply_fusion.3 = (f32[4096,512]{0,1:T(8,128)S(1)}, f32[4096,512]{0,1:T(8,128)S(1)}) fusion(), kind=kLoop, calls=%fused_computation.42 | loop fusion | flops 35651584 | bytes 16777216 | tf_op jit(solution)/shard_map/mul | solution.py:40
  36.9 0.0 copy-done.4
  36.9 0.1 fusion.53
  37.0 37.2 %cosine_multiply_fusion.2 = (f32[4096,512]{0,1:T(8,128)}, f32[4096,512]{0,1:T(8,128)}) fusion(s32[512]{0:T(512)S(1)} %iota_add_fusion.2), kind=kLoop, calls=%fused_computation.39 | loop fusion | flops 35651584 | bytes 16779264 | tf_op jit(solution)/shard_map/mul | solution.py:40
  74.3 37.2 %cosine_multiply_fusion.1 = (f32[4096,512]{0,1:T(8,128)}, f32[4096,512]{0,1:T(8,128)}) fusion(s32[512]{0:T(512)S(1)} %iota_add_fusion.1), kind=kLoop, calls=%fused_computation.35 | loop fusion | flops 35651584 | bytes 16779264 | tf_op jit(solution)/shard_map/mul | solution.py:40
  111.5 44.3 %cosine_multiply_fusion = (f32[4096,512]{0,1:T(8,128)S(1)}, f32[4096,512]{0,1:T(8,128)S(1)}) fusion(s32[512]{0:T(512)S(1)} %iota_add_fusion), kind=kLoop, calls=%fused_computation.31 | loop fusion | flops 35651584 | bytes 16779264 | tf_op jit(solution)/shard_map/mul | solution.py:40
  155.8 11.9 %pad_maximum_fusion.1 = f32[4096,1024]{0,1:T(8,128)} fusion(f32[4096,512]{0,1:T(8,128)} %get-tuple-element.14, f32[4096,512]{0,1:T(8,128)} %get-tuple-element.13), kind=kLoop, calls=%fused_computation.1 | loop fusion | flops 4194304 | bytes 33554432 | tf_op jit(solution)/shard_map/concatenate | solution.py:40
  167.7 11.9 %pad_maximum_fusion.2 = f32[4096,1024]{0,1:T(8,128)} fusion(f32[4096,512]{0,1:T(8,128)} %get-tuple-element.16, f32[4096,512]{0,1:T(8,128)} %get-tuple-element.15), kind=kLoop, calls=%fused_computation.2 | loop fusion | flops 4194304 | bytes 33554432 | tf_op jit(solution)/shard_map/concatenate | solution.py:40
  179.6 6.4 pad_maximum_fusion
  185.9 6.4 pad_maximum_fusion.3
  192.3 0.0 collective-permute-done
  192.3 5.6 multiply_add_fusion
  198.0 0.0 copy-start
  198.0 0.0 slice-start.1
  198.0 0.0 slice-start.2
  198.0 0.0 slice-start.3
  198.0 22.5 %fusion.38 = bf16[8,16,2,512]{3,1,2,0:T(8,128)(2,1)} fusion(f32[2,512,4096,1]{2,1,0,3:T(8,128)} %bitcast.82, f32[8,16,4096]{2,1,0:T(8,128)S(1)} %multiply_add_fusion), kind=kOutput, calls=%fused_computation.78 | convolution fusion | flops 6442582016 | bytes 19136512 | tf_op jit(solution)/shard_map/dot_general | solution.py:69
  220.5 0.0 copy-done
  220.5 0.0 slice-done
  220.6 0.0 copy-start.1
  220.6 0.0 slice-start.4
  220.6 0.0 slice-start.5
  220.6 20.0 %fusion.41 = bf16[8,16,2,512]{3,1,2,0:T(8,128)(2,1)} fusion(f32[2,512,4096,1]{2,1,0,3:T(8,128)S(1)} %bitcast.85, f32[8,16,4096]{2,1,0:T(8,128)} %copy-done), kind=kOutput, calls=%fused_computation.79 | convolution fusion | flops 6442582016 | bytes 19136512 | tf_op jit(solution)/shard_map/dot_general | solution.py:69
  240.6 20.8 %fusion.35 = bf16[8,16,2,512]{3,1,2,0:T(8,128)(2,1)S(1)} fusion(f32[2,512,4096,1]{2,1,0,3:T(8,128)} %bitcast.86, f32[8,16,4096]{2,1,0:T(8,128)S(1)} %copy-done.1), kind=kOutput, calls=%fused_computation.77 | convolution fusion | flops 6442582016 | bytes 19136512 | tf_op jit(solution)/shard_map/dot_general | solution.py:69
  261.5 17.6 %fusion.44 = bf16[8,16,2,512]{3,1,2,0:T(8,128)(2,1)S(1)} fusion(f32[2,512,4096,1]{2,1,0,3:T(8,128)S(1)} %bitcast.89, f32[8,16,4096]{2,1,0:T(8,128)S(1)} %copy-done.1), kind=kOutput, calls=%fused_computation.80 | convolution fusion | flops 6442582016 | bytes 19136512 | tf_op jit(solution)/shard_map/dot_general | solution.py:69
  279.1 0.0 copy-done.2
  279.1 0.0 copy-done.3
  279.1 0.1 pad_maximum_fusion.5
  279.2 14.3 %copy.32 = bf16[8,16,2,2048]{1,2,0,3:T(2,128)(2,1)} copy(bf16[8,16,2,2048]{3,1,2,0:T(8,128)(2,1)S(1)} %pad_maximum_fusion.5) | data formatting | bytes 2097152 | tf_op jit(solution)/shard_map/concatenate | solution.py:77
  293.5 10.2 reshape.96
  303.8 15.8 %all_to_all.20 = bf16[4,2,65536]{2,1,0:T(2,128)(2,1)S(1)} all-to-all(bf16[4,2,65536]{2,1,0:T(2,128)(2,1)S(1)} %reshape.96), channel_id=1, replica_groups=mesh['chan'=4,'blk'=32] {'chan'}, dimensions={0} | all-to-all | bytes 2097152 | tf_op jit(solution)/shard_map/all_to_all | solution.py:79
  319.6 7.1 reshape.97
  326.7 19.1 %copy.43 = bf16[8,16,2,4,512]{4,3,1,2,0:T(4,128)(2,1)S(1)} copy(bf16[8,16,2,4,512]{1,2,0,4,3:T(2,128)(2,1)} %bitcast.81) | data formatting | bytes 2097152 | tf_op jit(solution)/shard_map/all_to_all | solution.py:79
  345.8 0.2 copy.34
  346.1 11.1 %stack.7 = bf16[32,8,64,2,512]{4,2,3,1,0:T(8,128)(2,1)} broadcast(bf16[8,64,2,512]{3,1,2,0:T(8,128)(2,1)S(1)} %bitcast.90), dimensions={1,2,3,4} | broadcast | bytes 34603008 | tf_op jit(solution)/shard_map/stack | solution.py:16
  357.2 10.3 all-to-all-start.1
  367.5 2.0 copy.42
  369.5 629.9 %all-to-all-done.1 = bf16[32,8,64,2,512]{4,2,3,1,0:T(8,128)(2,1)} async-done(((bf16[32,8,64,2,512]{4,2,3,1,0:T(8,128)(2,1)}), bf16[32,8,64,2,512]{4,2,3,1,0:T(8,128)(2,1)}, u32[]{:S(2)}, u32[]{:S(2)}) %all-to-all-start.1) | async-done | bytes 33554464 | tf_op jit(solution)/shard_map/all_to_all | solution.py:15
  999.4 50.8 %copy.41 = bf16[256,64,2,512,1]{0,1,4,2,3:T(8,128)(2,1)} copy(bf16[256,64,2,512,1]{3,1,2,0,4:T(8,128)(2,1)} %bitcast.28) | data formatting | bytes 67108864 | tf_op jit(solution)/shard_map/reshape | solution.py:14
  1050.1 18.9 %convolution_bitcast_fusion = f32[8,2,256,2,512]{2,0,1,3,4:T(8,128)} fusion(bf16[256,64,2,512,1]{0,1,4,2,3:T(8,128)(2,1)} %copy.41, bf16[8,64,2,512,1]{1,0,2,4,3:T(8,128)(2,1)S(1)} %copy.42), kind=kOutput, calls=%fused_computation.16 | convolution fusion | flops 536870912 | bytes 51380224 | tf_op jit(solution)/shard_map/itpc,jtqc->ipjqc/dot_general | solution.py:44
  1069.0 4.0 fusion.24
  1073.0 4.0 fusion.26
  1077.0 3.8 maximum_multiply_fusion
  1080.9 9.9 copy.39
  (18 shorter events, 0.0 us)
Async XLA Ops:
  1.9 190.4 %collective-permute-start = (bf16[8,7,4096]{2,1,0:T(8,128)(2,1)S(1)}, bf16[8,7,4096]{2,1,0:T(8,128)(2,1)}, u32[]{:S(2)}, u32[]{:S(2)}) collective-permute-start(bf16[8,7,4096]{2,1,0:T(8,128)(2,1)S(1)} %slice.80), channel_id=1, source_target_pairs={{0,32},{32,64},{64,96},{1,33},{33,65},{65,97},{2,34},{34,66},{66,9... | collective-permute-start | bytes 1376264 | tf_op jit(solution)/shard_map/ppermute | solution.py:31
  3.9 33.0 %copy-start.4 = (f32[8,4096]{1,0:T(8,128)S(1)}, f32[8,4096]{1,0:T(8,128)}, u32[]{:S(2)}) copy-start(f32[8,4096]{1,0:T(8,128)} %param.3) | copy-start | bytes 393220
  192.3 28.2 %slice-start = ((s8[16777216]{0:T(1024)(128)(4,1)}), s8[4194304]{0:T(1024)(128)(4,1)S(1)}, s32[]{:S(2)}) async-start(s8[16777216]{0:T(1024)(128)(4,1)} %bitcast.83), calls=%async_computation.2 | async-start | bytes 8388608
  198.0 22.5 %copy-start = (f32[8,16,4096]{2,1,0:T(8,128)}, f32[8,16,4096]{2,1,0:T(8,128)S(1)}, u32[]{:S(2)}) copy-start(f32[8,16,4096]{2,1,0:T(8,128)S(1)} %multiply_add_fusion) | copy-start | bytes 6291460
  198.0 22.5 %slice-start.1 = ((s8[16777216]{0:T(1024)(128)(4,1)}), s8[4194304]{0:T(1024)(128)(4,1)S(1)}, s32[]{:S(2)}) async-start(s8[16777216]{0:T(1024)(128)(4,1)} %bitcast.83), calls=%async_computation.3 | async-start | bytes 8388608
  198.0 22.5 %slice-start.2 = ((s8[16777216]{0:T(1024)(128)(4,1)}), s8[4194304]{0:T(1024)(128)(4,1)S(1)}, s32[]{:S(2)}) async-start(s8[16777216]{0:T(1024)(128)(4,1)} %bitcast.83), calls=%async_computation.4 | async-start | bytes 8388608
  198.0 22.5 %slice-start.3 = ((s8[16777216]{0:T(1024)(128)(4,1)}), s8[4194304]{0:T(1024)(128)(4,1)S(1)}, s32[]{:S(2)}) async-start(s8[16777216]{0:T(1024)(128)(4,1)} %bitcast.83), calls=%async_computation.5 | async-start | bytes 8388608
  220.6 20.0 %copy-start.1 = (f32[8,16,4096]{2,1,0:T(8,128)S(1)}, f32[8,16,4096]{2,1,0:T(8,128)}, u32[]{:S(2)}) copy-start(f32[8,16,4096]{2,1,0:T(8,128)} %copy-done) | copy-start | bytes 6291460
  220.6 40.8 %slice-start.4 = ((s8[16777216]{0:T(1024)(128)(4,1)}), s8[4194304]{0:T(1024)(128)(4,1)S(1)}, s32[]{:S(2)}) async-start(s8[16777216]{0:T(1024)(128)(4,1)} %bitcast.87), calls=%async_computation.6 | async-start | bytes 8388608
  220.6 40.8 %slice-start.5 = ((s8[16777216]{0:T(1024)(128)(4,1)}), s8[4194304]{0:T(1024)(128)(4,1)S(1)}, s32[]{:S(2)}) async-start(s8[16777216]{0:T(1024)(128)(4,1)} %bitcast.87), calls=%async_computation.7 | async-start | bytes 8388608
  240.6 20.8 %slice-start.6 = ((s8[16777216]{0:T(1024)(128)(4,1)}), s8[4194304]{0:T(1024)(128)(4,1)S(1)}, s32[]{:S(2)}) async-start(s8[16777216]{0:T(1024)(128)(4,1)} %bitcast.87), calls=%async_computation.8 | async-start | bytes 8388608
  240.6 20.8 %slice-start.7 = ((s8[16777216]{0:T(1024)(128)(4,1)}), s8[4194304]{0:T(1024)(128)(4,1)S(1)}, s32[]{:S(2)}) async-start(s8[16777216]{0:T(1024)(128)(4,1)} %bitcast.87), calls=%async_computation.9 | async-start | bytes 8388608
  261.4 17.6 %copy-start.2 = (bf16[8,16,2,512]{3,1,2,0:T(8,128)(2,1)S(1)}, bf16[8,16,2,512]{3,1,2,0:T(8,128)(2,1)}, u32[]{:S(2)}) copy-start(bf16[8,16,2,512]{3,1,2,0:T(8,128)(2,1)} %fusion.38) | copy-start | bytes 786436
  261.4 17.6 %copy-start.3 = (bf16[8,16,2,512]{3,1,2,0:T(8,128)(2,1)S(1)}, bf16[8,16,2,512]{3,1,2,0:T(8,128)(2,1)}, u32[]{:S(2)}) copy-start(bf16[8,16,2,512]{3,1,2,0:T(8,128)(2,1)} %fusion.41) | copy-start | bytes 786436
  357.2 642.2 %all-to-all-start.1 = ((bf16[32,8,64,2,512]{4,2,3,1,0:T(8,128)(2,1)}), bf16[32,8,64,2,512]{4,2,3,1,0:T(8,128)(2,1)}, u32[]{:S(2)}, u32[]{:S(2)}) async-start(bf16[32,8,64,2,512]{4,2,3,1,0:T(8,128)(2,1)} %stack.7), calls=%async_computation.1 | async-start | bytes 67108864 | tf_op jit(solution)/shard_map/all_to_all | solution.py:15
